TPU v7x, 32 devices: a whole 2x2x4 slice. The times are simulated.
32 devices in a mesh: groups: 2 (over y), dp: 4 (over z), tensor: 2 (over x), layer: 2 (over core).
Axes of the slice: x: 2, y: 2, z: 4, core: 2. Of those that a mesh axis runs over, the one named last changes fastest.
Arguments:
- hidden_in: bfloat16 [2, 8, 512, 14336], P('layer', ('groups', 'dp'), None, 'tensor'), parts along dimension 1, may hold values from -6 to 6
- out_grad: bfloat16 [2, 8, 512, 4096], P('layer', ('groups', 'dp'), 'tensor'), parts along dimension 1, may hold values from -6 to 6
- proj_in: bfloat16 [2, 14336, 64], P('layer', 'tensor'), may hold values from -0.046875 to 0.046875
- proj_out: bfloat16 [2, 4096, 64], P('layer'), may hold values from -0.09375 to 0.09375
- query_grads: bfloat16 [2, 1024, 4096], P('layer', 'dp', 'tensor'), may hold values from -1.5 to 1.5
- lengths: int32 [8], P(('groups', 'dp')), parts along dimension 0, may hold values from 128 to 512, as said below
- query_decision: int32 [1024], P('dp'), may hold values from 0 to 1023
Outputs:
- influence: float32 [8, 1024], P(('groups', 'dp')), parts along dimension 0
There are 2 independent parts, one for each index of `groups`. A program takes and returns all parts, laid end to end along the dimension named above; an argument that names none is the same for every part. Nothing has to cross between parts.
Inputs may be any that keep to these rules, and one draw needn't show every extreme that they name: `lengths`: in each part one transcript has all 512 tokens live and another has exactly 128.
All inputs are finite; a program needn't handle non-finite values.
Results may differ from a plain program's by a relative error of at most 0.004.
Values may be sent and summed in bfloat16 or wider, within the bound.
No kernel may reach another device: no remote copies, remote signals or barrier semaphores. Data moves between devices by JAX's collectives and lax.ppermute only.
A program may use at most 64 MiB of HBM per device.

v0:
```python
import jax
import jax.numpy as jnp
from jax import lax
from jax.sharding import PartitionSpec as P

DECISIONS = 1024


def decision_table(decisions):
    return (decisions[:, None] == jnp.arange(DECISIONS, dtype=jnp.int32)[None, :]).astype(
        jnp.float32
    )


def body(hidden_in, out_grad, proj_in, proj_out, query_grads, lengths, query_decision):
    hidden_rows = hidden_in[0]
    grad_rows = out_grad[0]
    side_hidden = proj_in[0]
    side_width = proj_out[0]
    query_rows = query_grads[0]
    ex_count = hidden_rows.shape[0]
    seq_shard = grad_rows.shape[1]
    first_pos = lax.axis_index("tensor") * seq_shard
    positions = first_pos + jnp.arange(seq_shard, dtype=jnp.int32)
    live_tokens = (positions[None, :] < lengths[:, None]).astype(jnp.float32)
    right = jnp.einsum("etd,dp->etp", grad_rows, side_width, preferred_element_type=jnp.float32)
    right = (right * live_tokens[:, :, None]).astype(jnp.bfloat16)
    left = jnp.einsum("etf,fp->etp", hidden_rows, side_hidden, preferred_element_type=jnp.float32)
    left_own = lax.psum_scatter(left, "tensor", scatter_dimension=1, tiled=True)
    partial_value = jnp.einsum(
        "etp,etq->epq", left_own, right.astype(jnp.float32), precision=lax.Precision.HIGHEST
    )
    partial_value = partial_value / lengths.astype(jnp.float32)[:, None, None]
    grad_part = lax.psum_scatter(partial_value, "tensor", scatter_dimension=1, tiled=True)
    grad_flat = grad_part.reshape(ex_count, -1).astype(jnp.bfloat16)
    block_rows = lax.all_gather(query_rows, "dp", axis=0, tiled=True)
    block_decisions = lax.all_gather(query_decision, "dp", axis=0, tiled=True)
    scores = jnp.einsum("ek,qk->eq", grad_flat, block_rows, preferred_element_type=jnp.float32)
    partial_dec = jnp.dot(scores, decision_table(block_decisions), precision=lax.Precision.HIGHEST)
    result = lax.psum(partial_dec, ("tensor", "layer"))
    return result


def solution(mesh):
    in_specs = (
        P("layer", ("groups", "dp"), None, "tensor"),
        P("layer", ("groups", "dp"), "tensor", None),
        P("layer", "tensor", None),
        P("layer", None, None),
        P("layer", "dp", "tensor"),
        P(("groups", "dp")),
        P("dp"),
    )
    out_specs = P(("groups", "dp"), None)
    return jax.shard_map(body, mesh=mesh, in_specs=in_specs, out_specs=out_specs, check_vma=False)
```

profile of v0, /device:TPU:0, one launch (start us, length us, event | category | flops | bytes accessed | tf_op | source)
XLA Modules:
  0.0 130.6 jit_solution(11717772726066423702)
XLA Ops:
  7.4 0.0 copy-start
  7.4 0.0 copy-start.2
  7.4 0.0 copy-start.1
  7.4 0.0 reduce-scatter.3.cloned.1.call-start
  7.4 6.4 %fusion.11 = f32[1,512,64]{1,2,0:T(8,128)} fusion(bf16[1,1,512,7168]{3,2,1,0:T(8,128)(2,1)} %param.7, bf16[1,7168,64]{1,2,0:T(8,128)(2,1)} %param.9), kind=kOutput, calls=%fused_computation.10 | convolution fusion | flops 469762048 | bytes 8388608 | tf_op jit(solution)/shard_map/etf,fp->etp/dot_general | solution.py:28
  13.8 0.0 reduce-scatter.3.cloned.1.call-update
  13.8 0.0 reduce-scatter.5.cloned.1.call-start
  14.5 0.0 copy-done
  14.5 0.0 copy-done.2
  14.6 0.7 fusion.14
  15.2 11.8 %reduce-scatter.3.cloned.1.call-done = f32[1,256,64]{1,2,0:T(8,128)} async-done(((f32[1,512,64]{1,2,0:T(8,128)}), f32[1,256,64]{1,2,0:T(8,128)}) %reduce-scatter.3.cloned.1.call-update) | async-done | bytes 65552 | tf_op jit(solution)/shard_map/reduce_scatter | solution.py:29
  27.1 1.6 %fusion.17 = f32[1,64,64]{2,1,0:T(8,128)} fusion(bf16[256,64]{1,0:T(8,128)(2,1)S(1)} %fusion.14, f32[1,256,64]{1,2,0:T(8,128)} %reduce-scatter.3.cloned.1.call-done, f32[]{:T(128)} %bitcast.7), kind=kOutput, calls=%fused_computation.13 | convolution fusion | flops 12587008 | bytes 114692 | tf_op jit(solution)/shard_map/etp,etq->epq/dot_general | solution.py:30
  28.7 0.0 reduce-scatter.5.cloned.1.call-update
  28.7 0.0 all-gather.4.cloned.1.call-start
  28.7 0.5 all-gather.4.cloned.1.call-update
  29.3 0.0 copy-done.1
  29.3 10.9 %all-gather.1 = s32[4,1,256]{2,1,0:T(1,128)S(1)} all-gather(s32[1,1,256]{2,1,0:T(1,128)S(1)} %bitcast.43), channel_id=1, replica_groups=mesh['groups'=2,'dp'=4,'tensor'=2,'layer'=2] {'dp'}, dimensions={0}, use_global_device_ids=true | all-gather | bytes 5120 | tf_op jit(solution)/shard_map/all_gather | solution.py:37
  40.2 0.0 reduce-scatter.5.cloned.1.call-done
  40.2 0.7 convert_element_type.30
  40.9 0.1 reshape.54
  41.0 70.4 %all-gather.4.cloned.1.call-done = bf16[1,1024,2048]{2,1,0:T(8,128)(2,1)} async-done(((bf16[1,256,2048]{2,1,0:T(8,128)(2,1)}), bf16[1,1024,2048]{2,1,0:T(8,128)(2,1)}) %all-gather.4.cloned.1.call-update) | async-done | bytes 4194320 | tf_op jit(solution)/shard_map/all_gather | solution.py:36
  111.4 3.4 %fusion.18 = f32[1024,1]{0,1:T(1,128)S(1)} fusion(bf16[2048,1]{0,1:T(2,128)(2,1)S(1)} %reshape.54, bf16[1,1024,2048]{2,1,0:T(8,128)(2,1)} %all-gather.4.cloned.1.call-done), kind=kOutput, calls=%fused_computation.14 | convolution fusion | flops 4194304 | bytes 4202496 | tf_op jit(solution)/shard_map/ek,qk->eq/dot_general | solution.py:38
  114.7 1.5 %fusion.4 = f32[1,1024]{1,0:T(1,128)S(1)} fusion(f32[1024,1]{0,1:T(1,128)S(1)} %fusion.18, s32[1024]{0:T(1024)S(1)} %bitcast.42), kind=kOutput, calls=%fused_computation.5 | convolution fusion | flops 13631488 | bytes 12288 | tf_op jit(solution)/shard_map/dot_general | solution.py:39
  116.2 7.0 %psum.7 = f32[1,1024]{1,0:T(1,128)} all-reduce(f32[1,1024]{1,0:T(1,128)S(1)} %fusion.4), channel_id=1, replica_groups=mesh['groups'=2,'dp'=4,'tensor'=2,'layer'=2] {'tensor','layer'}, use_global_device_ids=true, to_apply=%region_2.0 | all-reduce | flops 1024 | bytes 8192 | tf_op jit(solution)/shard_map/psum | solution.py:40
  (1 shorter events, 0.0 us)
Async XLA Ops:
  7.4 7.2 %copy-start = (bf16[1,1,256,4096]{3,2,1,0:T(8,128)(2,1)S(1)}, bf16[1,1,256,4096]{3,2,1,0:T(8,128)(2,1)}, u32[]{:S(2)}) copy-start(bf16[1,1,256,4096]{3,2,1,0:T(8,128)(2,1)} %param.8) | copy-start | bytes 6291460
  7.4 7.2 %copy-start.2 = (bf16[1,4096,64]{1,2,0:T(8,128)(2,1)S(1)}, bf16[1,4096,64]{1,2,0:T(8,128)(2,1)}, u32[]{:S(2)}) copy-start(bf16[1,4096,64]{1,2,0:T(8,128)(2,1)} %param.10) | copy-start | bytes 1572868
  7.4 21.9 %copy-start.1 = (s32[256]{0:T(256)S(1)}, s32[256]{0:T(256)}, u32[]{:S(2)}) copy-start(s32[256]{0:T(256)} %param.13) | copy-start | bytes 3076
  7.4 19.7 %reduce-scatter.3.cloned.1.call-start = ((), (), s32[]{:S(2)}) async-start(), calls=%async_computation.2 | async-start | bytes 196608 | tf_op jit(solution)/shard_map/reduce_scatter | solution.py:29
  13.8 26.4 %reduce-scatter.5.cloned.1.call-start = ((), (), s32[]{:S(2)}) async-start(), calls=%async_computation.3 | async-start | bytes 49152 | tf_op jit(solution)/shard_map/reduce_scatter | solution.py:34
  28.7 82.7 %all-gather.4.cloned.1.call-start = ((), (), s32[]{:S(2)}) async-start(), calls=%async_computation.4 | async-start | bytes 5242880 | tf_op jit(solution)/shard_map/all_gather | solution.py:36
Sparse Core Ops, SparseCore 0:
  13.9 13.0 reduce-scatter.2
  29.2 9.9 reduce-scatter.4
Sparse Core Ops, SparseCore 1:
  30.7 80.6 all-gather.3
where the time goes:
time: 131 us
  waiting for transfers between devices  82.7 us (63%)
  blocking collectives  17.9 us (14%)
  between operations  15.5 us (12%)
  matrix products  13.5 us (10%)
    all_gather x1, waiting for transfers between devices, body(): block_rows = lax.all_gather(query_rows, 'dp', axis=0, tiled=True)  70.4 us
    reduce_scatter x1, waiting for transfers between devices, body(): left_own = lax.psum_scatter(left, 'tensor', scatter_dimension=1, tiled=True)  11.8 us
    all_gather x1, blocking collectives, body(): block_decisions = lax.all_gather(query_decision, 'dp', axis=0, tiled=True)  10.9 us
    psum x1, blocking collectives, body(): result = lax.psum(partial_dec, ('tensor', 'layer'))  6.99 us
    dot_general x1, matrix products, body(): jnp.einsum('etf,fp->etp', hidden_rows, side_hidden, preferred_element_typ...  6.41 us
    dot_general x1, matrix products, body(): jnp.einsum('ek,qk->eq', grad_flat, block_rows, preferred_element_type=jnp...  3.37 us
  transfers between devices with their start and end apart: 3, of which 2 were waited for; matrix products, arithmetic and copies ran while one was open for 1% of the time, Pallas kernels for 0%

commit v1 on v0

--- a/solution.py
+++ b/solution.py
@@ -37,7 +37,7 @@
     block_decisions = lax.all_gather(query_decision, "dp", axis=0, tiled=True)
     scores = jnp.einsum("ek,qk->eq", grad_flat, block_rows, preferred_element_type=jnp.float32)
     partial_dec = jnp.dot(scores, decision_table(block_decisions), precision=lax.Precision.HIGHEST)
-    result = lax.psum(partial_dec, ("tensor", "layer"))
+    result = jnp.sum(lax.all_gather(partial_dec, ("tensor", "layer")), axis=0)
     return result
 
 

time: 131 us -> 130 us (level)
  blocking collectives: 17.9 us -> 16.1 us
    psum x1 -> x0, blocking collectives: 6.99 us -> none  [body(): result = lax.psum(partial_dec, ('tensor', 'layer'))]
    all_gather x0 -> x1, blocking collectives: none -> 5.2 us  [body(): result = jnp.sum(lax.all_gather(partial_dec, ('tensor', 'layer')), axis=0)]
where the time goes in v1:
time: 130 us; the launch traced here: 129 us
  waiting for transfers between devices  82.7 us (64%)
  blocking collectives  16.1 us (12%)
  between operations  15.5 us (12%)
  matrix products  13.6 us (10%)
  other arithmetic  1.34 us (1%)
    all_gather x1, waiting for transfers between devices, body(): block_rows = lax.all_gather(query_rows, 'dp', axis=0, tiled=True)  70.4 us
    reduce_scatter x1, waiting for transfers between devices, body(): left_own = lax.psum_scatter(left, 'tensor', scatter_dimension=1, tiled=True)  11.7 us
    all_gather x1, blocking collectives, body(): block_decisions = lax.all_gather(query_decision, 'dp', axis=0, tiled=True)  10.9 us
    dot_general x1, matrix products, body(): jnp.einsum('etf,fp->etp', hidden_rows, side_hidden, preferred_element_typ...  6.41 us
    all_gather x1, blocking collectives, body(): result = jnp.sum(lax.all_gather(partial_dec, ('tensor', 'layer')), axis=0)  5.2 us
    dot_general x1, matrix products, body(): jnp.einsum('ek,qk->eq', grad_flat, block_rows, preferred_element_type=jnp...  3.37 us
  transfers between devices with their start and end apart: 3, of which 2 were waited for; matrix products, arithmetic and copies ran while one was open for 1% of the time, Pallas kernels for 0%

profile of v1, /device:TPU:0, one launch (start us, length us, event | category | flops | bytes accessed | tf_op | source)
XLA Modules:
  0.0 129.5 jit_solution(596049260678587090)
XLA Ops:
  7.4 0.0 copy-start
  7.4 0.0 copy-start.1
  7.4 0.0 copy-start.2
  7.4 0.0 reduce-scatter.3.cloned.1.call-start
  7.4 6.4 %fusion.8 = f32[1,512,64]{1,2,0:T(8,128)} fusion(bf16[1,1,512,7168]{3,2,1,0:T(8,128)(2,1)} %param.7, bf16[1,7168,64]{1,2,0:T(8,128)(2,1)} %param.9), kind=kOutput, calls=%fused_computation.9 | convolution fusion | flops 469762048 | bytes 8388608 | tf_op jit(solution)/shard_map/etf,fp->etp/dot_general | solution.py:28
  13.8 0.0 reduce-scatter.3.cloned.1.call-update
  13.8 0.0 reduce-scatter.5.cloned.1.call-start
  14.5 0.0 copy-done
  14.5 0.0 copy-done.1
  14.6 0.8 fusion.14
  15.3 11.7 %reduce-scatter.3.cloned.1.call-done = f32[1,256,64]{1,2,0:T(8,128)} async-done(((f32[1,512,64]{1,2,0:T(8,128)}), f32[1,256,64]{1,2,0:T(8,128)}) %reduce-scatter.3.cloned.1.call-update) | async-done | bytes 65552 | tf_op jit(solution)/shard_map/reduce_scatter | solution.py:29
  27.1 1.6 %fusion.17 = f32[1,64,64]{2,1,0:T(8,128)} fusion(bf16[256,64]{0,1:T(8,128)(2,1)S(1)} %fusion.14, f32[1,256,64]{1,2,0:T(8,128)} %reduce-scatter.3.cloned.1.call-done, f32[]{:T(128)} %bitcast.7), kind=kOutput, calls=%fused_computation.13 | convolution fusion | flops 12587008 | bytes 114692 | tf_op jit(solution)/shard_map/etp,etq->epq/dot_general | solution.py:30
  28.7 0.0 reduce-scatter.5.cloned.1.call-update
  28.7 0.0 all-gather.5.cloned.1.call-start
  28.7 0.5 all-gather.5.cloned.1.call-update
  29.3 0.0 copy-done.2
  29.3 10.9 %all-gather.2 = s32[4,1,256]{2,1,0:T(1,128)S(1)} all-gather(s32[1,1,256]{2,1,0:T(1,128)S(1)} %bitcast.45), channel_id=1, replica_groups=mesh['groups'=2,'dp'=4,'tensor'=2,'layer'=2] {'dp'}, dimensions={0}, use_global_device_ids=true | all-gather | bytes 5120 | tf_op jit(solution)/shard_map/all_gather | solution.py:37
  40.2 0.0 reduce-scatter.5.cloned.1.call-done
  40.2 0.7 convert_element_type.30
  40.9 0.1 reshape.58
  41.0 70.4 %all-gather.5.cloned.1.call-done = bf16[1,1024,2048]{2,1,0:T(8,128)(2,1)} async-done(((bf16[1,256,2048]{2,1,0:T(8,128)(2,1)}), bf16[1,1024,2048]{2,1,0:T(8,128)(2,1)}) %all-gather.5.cloned.1.call-update) | async-done | bytes 4194320 | tf_op jit(solution)/shard_map/all_gather | solution.py:36
  111.4 3.4 %fusion.18 = f32[1024,1]{0,1:T(1,128)S(1)} fusion(bf16[2048,1]{0,1:T(2,128)(2,1)S(1)} %reshape.58, bf16[1,1024,2048]{2,1,0:T(8,128)(2,1)} %all-gather.5.cloned.1.call-done), kind=kOutput, calls=%fused_computation.14 | convolution fusion | flops 4194304 | bytes 4202496 | tf_op jit(solution)/shard_map/ek,qk->eq/dot_general | solution.py:38
  114.8 1.5 %fusion.4 = f32[1,1024]{1,0:T(1,128)S(1)} fusion(f32[1024,1]{0,1:T(1,128)S(1)} %fusion.18, s32[1024]{0:T(1024)S(1)} %bitcast.44), kind=kOutput, calls=%fused_computation.5 | convolution fusion | flops 13631488 | bytes 12288 | tf_op jit(solution)/shard_map/dot_general | solution.py:39
  116.2 5.2 %all-gather.1 = f32[4096]{0:T(1024)S(1)} all-gather(f32[1024]{0:T(1024)S(1)} %bitcast.43), channel_id=3, replica_groups=mesh['groups'=2,'dp'=4,'tensor'=2,'layer'=2] {'tensor','layer'}, dimensions={0}, use_global_device_ids=true | all-gather | bytes 20480 | tf_op jit(solution)/shard_map/all_gather | solution.py:40
  121.4 0.6 reduce.1
  (2 shorter events, 0.0 us)
Async XLA Ops:
  7.4 7.2 %copy-start = (bf16[1,1,256,4096]{3,2,1,0:T(8,128)(2,1)S(1)}, bf16[1,1,256,4096]{3,2,1,0:T(8,128)(2,1)}, u32[]{:S(2)}) copy-start(bf16[1,1,256,4096]{3,2,1,0:T(8,128)(2,1)} %param.8) | copy-start | bytes 6291460
  7.4 7.2 %copy-start.1 = (bf16[1,4096,64]{1,2,0:T(8,128)(2,1)S(1)}, bf16[1,4096,64]{1,2,0:T(8,128)(2,1)}, u32[]{:S(2)}) copy-start(bf16[1,4096,64]{1,2,0:T(8,128)(2,1)} %param.10) | copy-start | bytes 1572868
  7.4 21.9 %copy-start.2 = (s32[256]{0:T(256)S(1)}, s32[256]{0:T(256)}, u32[]{:S(2)}) copy-start(s32[256]{0:T(256)} %param.13) | copy-start | bytes 3076
  7.4 19.7 %reduce-scatter.3.cloned.1.call-start = ((), (), s32[]{:S(2)}) async-start(), calls=%async_computation.2 | async-start | bytes 196608 | tf_op jit(solution)/shard_map/reduce_scatter | solution.py:29
  13.8 26.4 %reduce-scatter.5.cloned.1.call-start = ((), (), s32[]{:S(2)}) async-start(), calls=%async_computation.3 | async-start | bytes 49152 | tf_op jit(solution)/shard_map/reduce_scatter | solution.py:34
  28.7 82.7 %all-gather.5.cloned.1.call-start = ((), (), s32[]{:S(2)}) async-start(), calls=%async_computation.4 | async-start | bytes 5242880 | tf_op jit(solution)/shard_map/all_gather | solution.py:36
Sparse Core Ops, SparseCore 0:
  13.9 13.0 reduce-scatter.2
  29.2 9.9 reduce-scatter.4
Sparse Core Ops, SparseCore 1:
  30.7 80.6 all-gather.4
